TPU v7x, 512 devices: a whole 4x8x8 slice. The times are simulated.
512 devices in a mesh: az: 64 (over z, y_lo, core), rad: 8 (over y_hi, x).
Axes of the slice: x: 4, y: 8 (y_hi: 2, y_lo: 4; y = y_hi * 4 + y_lo), z: 8, core: 2. Of those that a mesh axis runs over, the one named last changes fastest.
Arguments:
- density: float32 [1024, 384, 128], P('az', 'rad'), may hold values from 0.5 to 1.5
- flow_vars: float32 [4, 1024, 384, 128], P(None, 'az', 'rad'), may hold values from -6 to 6
- blade_offset: int32 [4], replicated, may hold values from 0 to 4, as said below
- smooth_width: int32 [128], replicated, may hold values from 1 to 4, as said below
Outputs:
- mean_fields: float32 [5, 1024, 384, 128], P(None, 'az', 'rad')
- q_field: float32 [1024, 384, 128], P('az', 'rad')
Inputs may be any that keep to these rules, and one draw needn't show every extreme that they name: `blade_offset`: some blade's passage has the offset 4. `smooth_width`: some axial station uses the half-width 4.
All inputs are finite; a program needn't handle non-finite values.
Results may differ from a plain program's by a relative error of at most 0.00002.
Values sent between devices are 32-bit elements; how exact they have to be, the bound alone decides.
No kernel may reach another device: no remote copies, remote signals or barrier semaphores. Data moves between devices by JAX's collectives and lax.ppermute only.
A program may use at most 64 MiB of HBM per device.

v0:
```python
import math
import jax
import jax.numpy as jnp
from jax import lax
from jax.sharding import PartitionSpec as P

BLADES = 4
MAXOFF = 4
HW = 4
AZ = ("blade", "slab")


def passed_along(block, axis, distance):
    devices = range(lax.axis_size(axis))
    route = [((i - distance) % len(devices), i) for i in devices]
    return lax.ppermute(block, axis, route)


def extended(block, sides, width, periodic):
    for axis, dim in sides:
        count = lax.axis_size(axis)
        forward = [(i, i + 1) for i in range(count - 1)]
        if periodic:
            forward.append((count - 1, 0))
        backward = [(target, source) for source, target in forward]
        low = lax.ppermute(
            lax.slice_in_dim(block, block.shape[dim] - width, None, axis=dim), axis, forward
        )
        high = lax.ppermute(lax.slice_in_dim(block, 0, width, axis=dim), axis, backward)
        block = jnp.concatenate([low, block, high], axis=dim)
    return block


def smoothing_taps(smooth_width):
    spread = jnp.arange(-HW, HW + 1)
    width = smooth_width.astype(jnp.float32)
    square = (spread.astype(jnp.float32) ** 2)[:, None]
    weights = jnp.where(
        jnp.abs(spread)[:, None] <= smooth_width[None, :],
        jnp.exp(-0.5 * square / (width * width)[None, :]),
        0.0,
    )
    return weights / jnp.sum(weights, axis=0, keepdims=True)


def apply_taps(source, taps, length):
    total = jnp.zeros(source.shape[:1] + (length,) + source.shape[2:], jnp.float32)
    for turn in range(2 * HW + 1):
        total = total + taps[turn] * source[:, turn : turn + length]
    return total


def edge_rate(field, axis):
    count = field.shape[axis]
    upper = jnp.concatenate(
        [
            lax.slice_in_dim(field, 1, count, axis=axis),
            lax.slice_in_dim(field, count - 1, count, axis=axis),
        ],
        axis=axis,
    )
    lower = jnp.concatenate(
        [
            lax.slice_in_dim(field, 0, 1, axis=axis),
            lax.slice_in_dim(field, 0, count - 1, axis=axis),
        ],
        axis=axis,
    )
    places = jnp.arange(count)
    span = jnp.where((places == 0) | (places == count - 1), 1.0, 2.0).astype(field.dtype)
    layout = [1] * field.ndim
    layout[axis] = count
    return (upper - lower) / span.reshape(layout)


def swirl_measure(smoothed, az_rate, radial_rate, axial_rate, radius):
    tensor_aa = radial_rate[0]
    tensor_ab = (az_rate[0] - smoothed[1]) / radius
    tensor_ac = axial_rate[0]
    tensor_ba = radial_rate[1]
    tensor_bb = (az_rate[1] + smoothed[0]) / radius
    tensor_bc = axial_rate[1]
    tensor_ca = radial_rate[2]
    tensor_cb = az_rate[2] / radius
    tensor_cc = axial_rate[2]
    diagonal_part = tensor_aa * tensor_aa + tensor_bb * tensor_bb + tensor_cc * tensor_cc
    cross_part = tensor_ab * tensor_ba + tensor_ac * tensor_ca + tensor_bc * tensor_cb
    return -0.5 * (diagonal_part + 2.0 * cross_part)


def shards(density, flow_vars, blade_offset, smooth_width):
    cells = density.shape[0]
    rad_cells = density.shape[1]
    group = lax.axis_size("slab")
    blade = lax.axis_index("blade")
    own_offset = jnp.sum(jnp.where(jnp.arange(BLADES) == blade, blade_offset, 0))
    velocity = flow_vars[0:3]
    carried = jnp.concatenate([density[None], density[None] * velocity, flow_vars[3:4]], axis=0)
    ahead = passed_along(carried[:, :MAXOFF], AZ, -1)
    contribution = lax.dynamic_slice_in_dim(
        jnp.concatenate([carried, ahead], axis=1), own_offset, cells, 1
    )
    sector_part = lax.psum(contribution, "blade")
    behind = passed_along(sector_part[:, cells - MAXOFF :], AZ, 1)
    phase_sums = lax.dynamic_slice_in_dim(
        jnp.concatenate([behind, sector_part], axis=1), MAXOFF - own_offset, cells, 1
    )
    mean_fields = jnp.concatenate(
        [phase_sums[0:1] / BLADES, phase_sums[1:4] / phase_sums[0:1], phase_sums[4:5] / BLADES],
        axis=0,
    )
    fluctuation = velocity - mean_fields[1:4]
    taps = smoothing_taps(smooth_width)
    rimmed = extended(fluctuation, ((AZ, 1),), HW, True)
    smoothed = apply_taps(rimmed, taps, cells)
    az_side = extended(smoothed, ((AZ, 1),), 1, True)
    rad_side = extended(smoothed, (("rad", 2),), 1, False)
    dtheta = 2.0 * math.pi / (cells * lax.axis_size(AZ))
    az_rate = (az_side[:, 2:] - az_side[:, :-2]) / (2.0 * dtheta)
    total_rad = rad_cells * lax.axis_size("rad")
    rows = lax.axis_index("rad") * rad_cells + jnp.arange(rad_cells)
    upper = jnp.where((rows == total_rad - 1)[:, None], smoothed, rad_side[:, :, 2:])
    lower = jnp.where((rows == 0)[:, None], smoothed, rad_side[:, :, :-2])
    span = jnp.where((rows == 0) | (rows == total_rad - 1), 1.0, 2.0).astype(jnp.float32)
    radial_rate = (upper - lower) / span[:, None]
    axial_rate = edge_rate(smoothed, 3)
    radius = (total_rad / 2 + rows.astype(jnp.float32) + 0.5)[:, None]
    q_field = swirl_measure(smoothed, az_rate, radial_rate, axial_rate, radius)
    return (mean_fields, q_field)


def solution(mesh):
    az, rad = mesh.devices.shape
    split = jax.sharding.Mesh(
        mesh.devices.reshape(BLADES, az // BLADES, rad), ("blade", "slab", "rad")
    )
    in_specs = (P(AZ, "rad", None), P(None, AZ, "rad", None), P(), P())
    out_specs = (P(None, AZ, "rad", None), P(AZ, "rad", None))
    return jax.shard_map(
        shards, mesh=split, in_specs=in_specs, out_specs=out_specs, check_vma=False
    )
```

profile of v0, /device:TPU:32, one launch (start us, length us, event | category | flops | bytes accessed | tf_op | source)
XLA Modules:
  0.0 195.5 jit_solution(17805172556178679589)
XLA Ops:
  7.2 0.0 all-reduce.2.cloned.1.call-start
  7.2 1.0 slice.161
  8.2 0.0 copy-start.1
  8.2 1.5 slice_multiply_fusion
  9.8 0.0 copy-done.1
  9.8 0.0 copy-start.3
  9.8 10.7 %collective-permute-start = (f32[5,4,48,128]{3,2,1,0:T(8,128)S(1)}, f32[5,4,48,128]{3,2,1,0:T(8,128)S(1)}, u32[]{:S(2)}, u32[]{:S(2)}) collective-permute-start(f32[5,4,48,128]{3,2,1,0:T(8,128)S(1)} %pad_maximum_fusion.7), channel_id=1, source_target_pairs={{8,0},{16,8},{24,16},{32,24},{40,32},{48,40},{56,48},{64,56},{72,6... | collective-permute-start | bytes 1474568 | tf_op jit(solution)/shard_map/ppermute | solution.py:16
  20.6 0.0 copy-done.3
  20.6 0.6 fusion.54
  23.1 3.7 %collective-permute-done = f32[5,4,48,128]{3,2,1,0:T(8,128)S(1)} collective-permute-done((f32[5,4,48,128]{3,2,1,0:T(8,128)S(1)}, f32[5,4,48,128]{3,2,1,0:T(8,128)S(1)}, u32[]{:S(2)}, u32[]{:S(2)}) %collective-permute-start) | collective-permute-done | bytes 491552 | tf_op jit(solution)/shard_map/ppermute | solution.py:16
  26.9 1.5 fusion.3
  28.4 0.0 copy-start.2
  28.4 0.0 all-reduce.2.cloned.1.call-update
  28.5 0.6 copy-done.2
  29.1 0.1 fusion.53
  29.2 98.0 %all-reduce.2.cloned.1.call-done = f32[5,16,48,128]{3,2,1,0:T(8,128)} async-done(((f32[5,16,48,128]{3,2,1,0:T(8,128)}), f32[5,16,48,128]{3,2,1,0:T(8,128)}) %all-reduce.2.cloned.1.call-update) | async-done | bytes 1966096 | tf_op jit(solution)/shard_map/psum | solution.py:103
  127.1 1.1 slice.209
  128.2 1.9 collective-permute-start.1
  131.4 0.1 fusion.52
  131.5 10.7 %collective-permute-done.1 = f32[5,4,48,128]{3,2,1,0:T(8,128)S(1)} collective-permute-done((f32[5,4,48,128]{3,2,1,0:T(8,128)S(1)}, f32[5,4,48,128]{3,2,1,0:T(8,128)S(1)}, u32[]{:S(2)}, u32[]{:S(2)}) %collective-permute-start.1) | collective-permute-done | bytes 491552 | tf_op jit(solution)/shard_map/ppermute | solution.py:16
  142.3 1.6 fusion
  143.8 0.0 copy-start
  143.8 0.1 slice_multiply_fusion.5
  143.9 1.3 copy-done
  145.2 0.3 slice_subtract_fusion
  145.6 1.9 collective-permute-start.2
  147.5 7.5 %collective-permute-start.3 = (f32[3,4,48,128]{3,2,1,0:T(8,128)S(1)}, f32[3,4,48,128]{3,2,1,0:T(8,128)S(1)}, u32[]{:S(2)}, u32[]{:S(2)}) collective-permute-start(f32[3,4,48,128]{3,2,1,0:T(8,128)S(1)} %get-tuple-element.18), channel_id=1, source_target_pairs={{8,0},{16,8},{24,16},{32,24},{40,32},{48,40},{56,48},{64,56},{72,6... | collective-permute-start | bytes 884744 | tf_op jit(solution)/shard_map/ppermute | solution.py:29
  155.1 1.5 pad_maximum_fusion
  156.5 1.6 collective-permute-done.2
  158.2 1.1 collective-permute-done.3
  159.3 1.1 fusion.7
  160.4 0.4 fusion.59
  160.8 0.4 fusion.60
  161.2 7.7 %collective-permute-start.6 = (f32[3,1,48,128]{3,2,1,0:T(8,128)S(1)}, f32[3,1,48,128]{3,2,1,0:T(8,128)S(1)}, u32[]{:S(2)}, u32[]{:S(2)}) collective-permute-start(f32[3,1,48,128]{3,2,1,0:T(8,128)S(1)} %get-tuple-element.15), channel_id=1, source_target_pairs={{8,0},{16,8},{24,16},{32,24},{40,32},{48,40},{56,48},{64,56},{72,6... | collective-permute-start | bytes 221192 | tf_op jit(solution)/shard_map/ppermute | solution.py:29
  168.9 1.9 collective-permute-start.7
  170.9 4.5 %collective-permute-start.4 = (f32[3,16,1,128]{3,2,1,0:T(1,128)S(1)}, f32[3,16,1,128]{3,2,1,0:T(1,128)S(1)}, u32[]{:S(2)}, u32[]{:S(2)}) collective-permute-start(f32[3,16,1,128]{3,2,1,0:T(1,128)S(1)} %get-tuple-element.9), channel_id=1, source_target_pairs={{1,0},{2,1},{3,2},{4,3},{5,4},{6,5},{7,6},{9,8},{10,9},{11,10},{12... | collective-permute-start | bytes 73736 | tf_op jit(solution)/shard_map/ppermute | solution.py:29
  175.4 1.9 collective-permute-start.5
  177.3 0.7 fusion.32
  178.0 0.0 collective-permute-done.4
  178.0 9.1 %collective-permute-done.5 = f32[3,16,1,128]{3,2,1,0:T(1,128)S(1)} collective-permute-done((f32[3,16,1,128]{3,2,1,0:T(1,128)S(1)}, f32[3,16,1,128]{3,2,1,0:T(1,128)S(1)}, u32[]{:S(2)}, u32[]{:S(2)}) %collective-permute-start.5) | collective-permute-done | bytes 24608 | tf_op jit(solution)/shard_map/ppermute | solution.py:26
  187.1 0.0 collective-permute-done.6
  187.1 0.0 collective-permute-done.7
  187.1 0.5 fusion.28
  187.6 1.1 fusion.38
  (11 shorter events, 0.2 us)
Async XLA Ops:
  7.2 120.0 %all-reduce.2.cloned.1.call-start = ((), (), s32[]{:S(2)}) async-start(), calls=%async_computation | async-start | bytes 3932160 | tf_op jit(solution)/shard_map/psum | solution.py:103
  8.2 1.5 copy-start.1
  9.8 10.8 %copy-start.3 = (s32[4]{0:T(128)S(1)}, s32[4]{0:T(128)}, u32[]{:S(2)}) copy-start(s32[4]{0:T(128)} %param.6) | copy-start | bytes 52
  9.8 17.1 %collective-permute-start = (f32[5,4,48,128]{3,2,1,0:T(8,128)S(1)}, f32[5,4,48,128]{3,2,1,0:T(8,128)S(1)}, u32[]{:S(2)}, u32[]{:S(2)}) collective-permute-start(f32[5,4,48,128]{3,2,1,0:T(8,128)S(1)} %pad_maximum_fusion.7), channel_id=1, source_target_pairs={{8,0},{16,8},{24,16},{32,24},{40,32},{48,40},{56,48},{64,56},{72,6... | collective-permute-start | bytes 1474568 | tf_op jit(solution)/shard_map/ppermute | solution.py:16
  28.4 0.7 copy-start.2
  128.2 14.1 %collective-permute-start.1 = (f32[5,4,48,128]{3,2,1,0:T(8,128)S(1)}, f32[5,4,48,128]{3,2,1,0:T(8,128)S(1)}, u32[]{:S(2)}, u32[]{:S(2)}) collective-permute-start(f32[5,4,48,128]{3,2,1,0:T(8,128)S(1)} %slice.209), channel_id=1, source_target_pairs={{504,0},{0,8},{8,16},{16,24},{24,32},{32,40},{40,48},{48,56},{56,6... | collective-permute-start | bytes 1474568 | tf_op jit(solution)/shard_map/ppermute | solution.py:16
  143.8 1.4 copy-start
  145.6 12.6 %collective-permute-start.2 = (f32[3,4,48,128]{3,2,1,0:T(8,128)S(1)}, f32[3,4,48,128]{3,2,1,0:T(8,128)S(1)}, u32[]{:S(2)}, u32[]{:S(2)}) collective-permute-start(f32[3,4,48,128]{3,2,1,0:T(8,128)S(1)} %get-tuple-element.17), channel_id=1, source_target_pairs={{0,8},{8,16},{16,24},{24,32},{32,40},{40,48},{48,56},{56,64},{64,7... | collective-permute-start | bytes 884744 | tf_op jit(solution)/shard_map/ppermute | solution.py:26
  147.5 11.8 %collective-permute-start.3 = (f32[3,4,48,128]{3,2,1,0:T(8,128)S(1)}, f32[3,4,48,128]{3,2,1,0:T(8,128)S(1)}, u32[]{:S(2)}, u32[]{:S(2)}) collective-permute-start(f32[3,4,48,128]{3,2,1,0:T(8,128)S(1)} %get-tuple-element.18), channel_id=1, source_target_pairs={{8,0},{16,8},{24,16},{32,24},{40,32},{48,40},{56,48},{64,56},{72,6... | collective-permute-start | bytes 884744 | tf_op jit(solution)/shard_map/ppermute | solution.py:29
  161.2 25.9 %collective-permute-start.6 = (f32[3,1,48,128]{3,2,1,0:T(8,128)S(1)}, f32[3,1,48,128]{3,2,1,0:T(8,128)S(1)}, u32[]{:S(2)}, u32[]{:S(2)}) collective-permute-start(f32[3,1,48,128]{3,2,1,0:T(8,128)S(1)} %get-tuple-element.15), channel_id=1, source_target_pairs={{8,0},{16,8},{24,16},{32,24},{40,32},{48,40},{56,48},{64,56},{72,6... | collective-permute-start | bytes 221192 | tf_op jit(solution)/shard_map/ppermute | solution.py:29
  168.9 18.2 %collective-permute-start.7 = (f32[3,1,48,128]{3,2,1,0:T(8,128)S(1)}, f32[3,1,48,128]{3,2,1,0:T(8,128)S(1)}, u32[]{:S(2)}, u32[]{:S(2)}) collective-permute-start(f32[3,1,48,128]{3,2,1,0:T(8,128)S(1)} %get-tuple-element.16), channel_id=1, source_target_pairs={{0,8},{8,16},{16,24},{24,32},{32,40},{40,48},{48,56},{56,64},{64,7... | collective-permute-start | bytes 221192 | tf_op jit(solution)/shard_map/ppermute | solution.py:26
  170.9 7.1 %collective-permute-start.4 = (f32[3,16,1,128]{3,2,1,0:T(1,128)S(1)}, f32[3,16,1,128]{3,2,1,0:T(1,128)S(1)}, u32[]{:S(2)}, u32[]{:S(2)}) collective-permute-start(f32[3,16,1,128]{3,2,1,0:T(1,128)S(1)} %get-tuple-element.9), channel_id=1, source_target_pairs={{1,0},{2,1},{3,2},{4,3},{5,4},{6,5},{7,6},{9,8},{10,9},{11,10},{12... | collective-permute-start | bytes 73736 | tf_op jit(solution)/shard_map/ppermute | solution.py:29
  175.4 11.7 %collective-permute-start.5 = (f32[3,16,1,128]{3,2,1,0:T(1,128)S(1)}, f32[3,16,1,128]{3,2,1,0:T(1,128)S(1)}, u32[]{:S(2)}, u32[]{:S(2)}) collective-permute-start(f32[3,16,1,128]{3,2,1,0:T(1,128)S(1)} %get-tuple-element.10), channel_id=1, source_target_pairs={{0,1},{1,2},{2,3},{3,4},{4,5},{5,6},{6,7},{8,9},{9,10},{10,11},{11... | collective-permute-start | bytes 73736 | tf_op jit(solution)/shard_map/ppermute | solution.py:26
Sparse Core Ops, SparseCore 0:
  28.6 98.5 all-reduce.1
where the time goes:
time: 196 us; the launch traced here: 195 us
  waiting for transfers between devices  124 us (63%)
  starting transfers between devices  38.2 us (19%)
  between operations  17.5 us (9%)
  other arithmetic  10.6 us (5%)
  local copies, waits for them, and re-layouts  4.86 us (2%)
    psum x1, waiting for transfers between devices, shards(): sector_part = lax.psum(contribution, 'blade')  98 us
    ppermute x3, starting transfers between devices, extended(): lax.ppermute(lax.slice_in_dim(block, 0, width, axis=dim), axis, backward)  19.8 us
    ppermute x2, waiting for transfers between devices, passed_along(): return lax.ppermute(block, axis, route)  14.5 us
    ppermute x2, starting transfers between devices, passed_along(): return lax.ppermute(block, axis, route)  12.6 us
    ppermute x3, waiting for transfers between devices, extended(): lax.ppermute(lax.slice_in_dim(block, block.shape[dim] - width, None, axis...  10.8 us
    ppermute x3, starting transfers between devices, extended(): lax.ppermute(lax.slice_in_dim(block, block.shape[dim] - width, None, axis...  5.76 us
  transfers between devices with their start and end apart: 9, of which 6 were waited for; matrix products, arithmetic and copies ran while one was open for 2% of the time, Pallas kernels for 0%

commit v1 on v0

--- a/solution.py
+++ b/solution.py
@@ -100,7 +100,11 @@
     contribution = lax.dynamic_slice_in_dim(
         jnp.concatenate([carried, ahead], axis=1), own_offset, cells, 1
     )
-    sector_part = lax.psum(contribution, "blade")
+
+    def _load_packet(mine_x, comm_axis="blade"):
+        return jax.lax.all_gather(mine_x, comm_axis).sum(axis=0)
+
+    sector_part = _load_packet(contribution)
     behind = passed_along(sector_part[:, cells - MAXOFF :], AZ, 1)
     phase_sums = lax.dynamic_slice_in_dim(
         jnp.concatenate([behind, sector_part], axis=1), MAXOFF - own_offset, cells, 1

time: 196 us -> 247 us (1.26)
  waiting for transfers between devices: 124 us -> 174 us
  other arithmetic: 10.6 us -> 13.3 us
    all_gather x0 -> x1, waiting for transfers between devices: none -> 148 us  [_load_packet(): return jax.lax.all_gather(mine_x, comm_axis).sum(axis=0)]
    psum x1 -> x0, waiting for transfers between devices: 98 us -> none  [shards(): sector_part = lax.psum(contribution, 'blade')]
    reduce_sum x0 -> x1, other arithmetic: none -> 3.97 us  [_load_packet(): return jax.lax.all_gather(mine_x, comm_axis).sum(axis=0)]
  transfers between devices with their start and end apart: 9 -> 9, of which waited for: 6 -> 6; matrix products, arithmetic and copies ran while one was open for 2% -> 1% of each run, Pallas kernels for 0% -> 0%
where the time goes in v1:
time: 247 us
  waiting for transfers between devices  174 us (70%)
  starting transfers between devices  38.2 us (15%)
  between operations  17.5 us (7%)
  other arithmetic  13.3 us (5%)
  local copies, waits for them, and re-layouts  3.83 us (2%)
    all_gather x1, waiting for transfers between devices, _load_packet(): return jax.lax.all_gather(mine_x, comm_axis).sum(axis=0)  148 us
    ppermute x3, starting transfers between devices, extended(): lax.ppermute(lax.slice_in_dim(block, 0, width, axis=dim), axis, backward)  19.8 us
    ppermute x2, waiting for transfers between devices, passed_along(): return lax.ppermute(block, axis, route)  14.5 us
    ppermute x2, starting transfers between devices, passed_along(): return lax.ppermute(block, axis, route)  12.6 us
    ppermute x3, waiting for transfers between devices, extended(): lax.ppermute(lax.slice_in_dim(block, block.shape[dim] - width, None, axis...  9.98 us
    ppermute x3, starting transfers between devices, extended(): lax.ppermute(lax.slice_in_dim(block, block.shape[dim] - width, None, axis...  5.76 us
  transfers between devices with their start and end apart: 9, of which 6 were waited for; matrix products, arithmetic and copies ran while one was open for 1% of the time, Pallas kernels for 0%

profile of v1, /device:TPU:32, one launch (start us, length us, event | category | flops | bytes accessed | tf_op | source)
XLA Modules:
  0.0 246.9 jit_solution(18016781431365652815)
XLA Ops:
  7.2 0.0 all-gather.3.cloned.1.call-start
  7.2 1.0 slice.161
  8.2 0.0 copy-start.1
  8.2 1.5 slice_multiply_fusion
  9.8 0.0 copy-done.1
  9.8 0.0 copy-start.3
  9.8 10.7 %collective-permute-start = (f32[5,4,48,128]{3,2,1,0:T(8,128)S(1)}, f32[5,4,48,128]{3,2,1,0:T(8,128)S(1)}, u32[]{:S(2)}, u32[]{:S(2)}) collective-permute-start(f32[5,4,48,128]{3,2,1,0:T(8,128)S(1)} %pad_maximum_fusion.7), channel_id=1, source_target_pairs={{8,0},{16,8},{24,16},{32,24},{40,32},{48,40},{56,48},{64,56},{72,6... | collective-permute-start | bytes 1474568 | tf_op jit(solution)/shard_map/ppermute | solution.py:16
  20.6 0.0 copy-done.3
  20.6 0.6 fusion.54
  23.1 3.7 %collective-permute-done = f32[5,4,48,128]{3,2,1,0:T(8,128)S(1)} collective-permute-done((f32[5,4,48,128]{3,2,1,0:T(8,128)S(1)}, f32[5,4,48,128]{3,2,1,0:T(8,128)S(1)}, u32[]{:S(2)}, u32[]{:S(2)}) %collective-permute-start) | collective-permute-done | bytes 491552 | tf_op jit(solution)/shard_map/ppermute | solution.py:16
  26.9 1.5 fusion.3
  28.4 0.0 copy-start.2
  28.4 0.0 all-gather.3.cloned.1.call-update
  28.5 0.6 copy-done.2
  29.1 0.1 fusion.53
  29.2 147.7 %all-gather.3.cloned.1.call-done = f32[20,16,48,128]{3,2,1,0:T(8,128)} async-done(((f32[5,16,48,128]{3,2,1,0:T(8,128)}), f32[20,16,48,128]{3,2,1,0:T(8,128)}) %all-gather.3.cloned.1.call-update) | async-done | bytes 7864336 | tf_op jit(solution)/shard_map/all_gather | solution.py:105
  176.9 4.0 %reduce_sum.28 = f32[5,16,48,128]{3,2,1,0:T(8,128)S(1)} reduce(f32[4,5,16,48,128]{4,3,2,1,0:T(8,128)} %bitcast.78, f32[]{:T(128)} %constant.21.clone.1), dimensions={0}, to_apply=%region_1.2 | reduce | flops 1474560 | bytes 9830404 | tf_op jit(solution)/shard_map/reduce_sum | solution.py:105
  180.9 1.9 collective-permute-start.1
  184.2 0.1 fusion.52
  184.2 10.7 %collective-permute-done.1 = f32[5,4,48,128]{3,2,1,0:T(8,128)S(1)} collective-permute-done((f32[5,4,48,128]{3,2,1,0:T(8,128)S(1)}, f32[5,4,48,128]{3,2,1,0:T(8,128)S(1)}, u32[]{:S(2)}, u32[]{:S(2)}) %collective-permute-start.1) | collective-permute-done | bytes 491552 | tf_op jit(solution)/shard_map/ppermute | solution.py:16
  195.0 0.2 fusion
  195.2 0.0 copy-start
  195.2 0.1 slice_multiply_fusion.5
  195.3 1.3 copy-done
  196.6 0.3 slice_subtract_fusion
  196.9 1.9 collective-permute-start.2
  198.9 7.5 %collective-permute-start.3 = (f32[3,4,48,128]{3,2,1,0:T(8,128)S(1)}, f32[3,4,48,128]{3,2,1,0:T(8,128)S(1)}, u32[]{:S(2)}, u32[]{:S(2)}) collective-permute-start(f32[3,4,48,128]{3,2,1,0:T(8,128)S(1)} %get-tuple-element.18), channel_id=1, source_target_pairs={{8,0},{16,8},{24,16},{32,24},{40,32},{48,40},{56,48},{64,56},{72,6... | collective-permute-start | bytes 884744 | tf_op jit(solution)/shard_map/ppermute | solution.py:29
  206.4 1.5 pad_maximum_fusion
  207.9 1.0 collective-permute-done.2
  208.9 1.8 collective-permute-done.3
  210.6 1.1 fusion.7
  211.7 0.4 fusion.59
  212.1 0.4 fusion.60
  212.6 7.8 %collective-permute-start.6 = (f32[3,1,48,128]{3,2,1,0:T(8,128)S(1)}, f32[3,1,48,128]{3,2,1,0:T(8,128)S(1)}, u32[]{:S(2)}, u32[]{:S(2)}) collective-permute-start(f32[3,1,48,128]{3,2,1,0:T(8,128)S(1)} %get-tuple-element.15), channel_id=1, source_target_pairs={{8,0},{16,8},{24,16},{32,24},{40,32},{48,40},{56,48},{64,56},{72,6... | collective-permute-start | bytes 221192 | tf_op jit(solution)/shard_map/ppermute | solution.py:29
  220.3 1.9 collective-permute-start.7
  222.3 4.5 %collective-permute-start.4 = (f32[3,16,1,128]{3,2,1,0:T(1,128)S(1)}, f32[3,16,1,128]{3,2,1,0:T(1,128)S(1)}, u32[]{:S(2)}, u32[]{:S(2)}) collective-permute-start(f32[3,16,1,128]{3,2,1,0:T(1,128)S(1)} %get-tuple-element.9), channel_id=1, source_target_pairs={{1,0},{2,1},{3,2},{4,3},{5,4},{6,5},{7,6},{9,8},{10,9},{11,10},{12... | collective-permute-start | bytes 73736 | tf_op jit(solution)/shard_map/ppermute | solution.py:29
  226.7 1.9 collective-permute-start.5
  228.7 0.8 fusion.32
  229.5 0.0 collective-permute-done.4
  229.5 9.0 %collective-permute-done.5 = f32[3,16,1,128]{3,2,1,0:T(1,128)S(1)} collective-permute-done((f32[3,16,1,128]{3,2,1,0:T(1,128)S(1)}, f32[3,16,1,128]{3,2,1,0:T(1,128)S(1)}, u32[]{:S(2)}, u32[]{:S(2)}) %collective-permute-start.5) | collective-permute-done | bytes 24608 | tf_op jit(solution)/shard_map/ppermute | solution.py:26
  238.5 0.0 collective-permute-done.6
  238.5 0.0 collective-permute-done.7
  238.5 0.5 fusion.28
  239.0 1.1 fusion.38
  (12 shorter events, 0.2 us)
Async XLA Ops:
  7.2 169.7 %all-gather.3.cloned.1.call-start = ((), (), s32[]{:S(2)}) async-start(), calls=%async_computation | async-start | bytes 9830400 | tf_op jit(solution)/shard_map/all_gather | solution.py:105
  8.2 1.5 copy-start.1
  9.8 10.8 %copy-start.3 = (s32[4]{0:T(128)S(1)}, s32[4]{0:T(128)}, u32[]{:S(2)}) copy-start(s32[4]{0:T(128)} %param.6) | copy-start | bytes 52
  9.8 17.1 %collective-permute-start = (f32[5,4,48,128]{3,2,1,0:T(8,128)S(1)}, f32[5,4,48,128]{3,2,1,0:T(8,128)S(1)}, u32[]{:S(2)}, u32[]{:S(2)}) collective-permute-start(f32[5,4,48,128]{3,2,1,0:T(8,128)S(1)} %pad_maximum_fusion.7), channel_id=1, source_target_pairs={{8,0},{16,8},{24,16},{32,24},{40,32},{48,40},{56,48},{64,56},{72,6... | collective-permute-start | bytes 1474568 | tf_op jit(solution)/shard_map/ppermute | solution.py:16
  28.4 0.7 copy-start.2
  180.9 14.1 %collective-permute-start.1 = (f32[5,4,48,128]{3,2,1,0:T(8,128)S(1)}, f32[5,4,48,128]{3,2,1,0:T(8,128)S(1)}, u32[]{:S(2)}, u32[]{:S(2)}) collective-permute-start(f32[5,4,48,128]{3,2,1,0:T(8,128)S(1)} %slice.209), channel_id=1, source_target_pairs={{504,0},{0,8},{8,16},{16,24},{24,32},{32,40},{40,48},{48,56},{56,6... | collective-permute-start | bytes 1474568 | tf_op jit(solution)/shard_map/ppermute | solution.py:16
  195.2 1.4 copy-start
  196.9 11.9 %collective-permute-start.2 = (f32[3,4,48,128]{3,2,1,0:T(8,128)S(1)}, f32[3,4,48,128]{3,2,1,0:T(8,128)S(1)}, u32[]{:S(2)}, u32[]{:S(2)}) collective-permute-start(f32[3,4,48,128]{3,2,1,0:T(8,128)S(1)} %get-tuple-element.17), channel_id=1, source_target_pairs={{0,8},{8,16},{16,24},{24,32},{32,40},{40,48},{48,56},{56,64},{64,7... | collective-permute-start | bytes 884744 | tf_op jit(solution)/shard_map/ppermute | solution.py:26
  198.9 11.8 %collective-permute-start.3 = (f32[3,4,48,128]{3,2,1,0:T(8,128)S(1)}, f32[3,4,48,128]{3,2,1,0:T(8,128)S(1)}, u32[]{:S(2)}, u32[]{:S(2)}) collective-permute-start(f32[3,4,48,128]{3,2,1,0:T(8,128)S(1)} %get-tuple-element.18), channel_id=1, source_target_pairs={{8,0},{16,8},{24,16},{32,24},{40,32},{48,40},{56,48},{64,56},{72,6... | collective-permute-start | bytes 884744 | tf_op jit(solution)/shard_map/ppermute | solution.py:29
  212.6 25.9 %collective-permute-start.6 = (f32[3,1,48,128]{3,2,1,0:T(8,128)S(1)}, f32[3,1,48,128]{3,2,1,0:T(8,128)S(1)}, u32[]{:S(2)}, u32[]{:S(2)}) collective-permute-start(f32[3,1,48,128]{3,2,1,0:T(8,128)S(1)} %get-tuple-element.15), channel_id=1, source_target_pairs={{8,0},{16,8},{24,16},{32,24},{40,32},{48,40},{56,48},{64,56},{72,6... | collective-permute-start | bytes 221192 | tf_op jit(solution)/shard_map/ppermute | solution.py:29
  220.3 18.2 %collective-permute-start.7 = (f32[3,1,48,128]{3,2,1,0:T(8,128)S(1)}, f32[3,1,48,128]{3,2,1,0:T(8,128)S(1)}, u32[]{:S(2)}, u32[]{:S(2)}) collective-permute-start(f32[3,1,48,128]{3,2,1,0:T(8,128)S(1)} %get-tuple-element.16), channel_id=1, source_target_pairs={{0,8},{8,16},{16,24},{24,32},{32,40},{40,48},{48,56},{56,64},{64,7... | collective-permute-start | bytes 221192 | tf_op jit(solution)/shard_map/ppermute | solution.py:26
  222.3 7.2 %collective-permute-start.4 = (f32[3,16,1,128]{3,2,1,0:T(1,128)S(1)}, f32[3,16,1,128]{3,2,1,0:T(1,128)S(1)}, u32[]{:S(2)}, u32[]{:S(2)}) collective-permute-start(f32[3,16,1,128]{3,2,1,0:T(1,128)S(1)} %get-tuple-element.9), channel_id=1, source_target_pairs={{1,0},{2,1},{3,2},{4,3},{5,4},{6,5},{7,6},{9,8},{10,9},{11,10},{12... | collective-permute-start | bytes 73736 | tf_op jit(solution)/shard_map/ppermute | solution.py:29
  226.7 11.7 %collective-permute-start.5 = (f32[3,16,1,128]{3,2,1,0:T(1,128)S(1)}, f32[3,16,1,128]{3,2,1,0:T(1,128)S(1)}, u32[]{:S(2)}, u32[]{:S(2)}) collective-permute-start(f32[3,16,1,128]{3,2,1,0:T(1,128)S(1)} %get-tuple-element.10), channel_id=1, source_target_pairs={{0,1},{1,2},{2,3},{3,4},{4,5},{5,6},{6,7},{8,9},{9,10},{10,11},{11... | collective-permute-start | bytes 73736 | tf_op jit(solution)/shard_map/ppermute | solution.py:26
Sparse Core Ops, SparseCore 0:
  28.6 148.2 all-gather.2
